TPU v7x, 512 devices: a whole 4x8x8 slice. The times are simulated.
512 devices in a mesh: band: 16 (over y, core), dom: 32 (over z, x).
Axes of the slice: x: 4, y: 8, z: 8, core: 2. Of those that a mesh axis runs over, the one named last changes fastest.
Arguments:
- orbitals: float32 [32, 2, 256, 8, 128], P('band', None, 'dom'), may hold values from -6 to 6
- ace_vectors: float32 [16, 2, 256, 8, 128], P(None, None, 'dom'), may hold values from -0.078125 to 0.078125
- local_potential: float32 [256, 8, 128], P('dom'), may hold values from -1 to 1
- field_strength: float32 [2], replicated, may hold values from -2 to 2
- run_projectors: float32 [1024, 4, 256], P('dom'), may hold values from -0.09375 to 0.09375
- run_atom: int32 [1024], P('dom'), may hold values from 0 to 127, as said below
- run_count: int32 [1024], P('dom'), may hold values from 1 to 256, as said below
- run_start: int32 [1024], P('dom'), may hold values from 0 to 7936, as said below
- kb_energy: float32 [128], P('dom'), may hold values from 0.1 to 1
Outputs:
- propagated: float32 [32, 2, 256, 8, 128], P('band', None, 'dom')
- forces: float32 [2, 3, 128], P(None, None, 'dom')
Inputs may be any that keep to these rules, and one draw needn't show every extreme that they name: `run_atom`: atom a is owned by index a // 4 of dom. The 32 runs of one dom index name atoms of any one owner at most 2 times, and exactly 2 times for some owner. `run_count`: every dom index has a run of 256 points. `run_start`: every dom index has a run that starts at cell 8192 - 256.
All inputs are finite; a program needn't handle non-finite values.
Results may differ from a plain program's by a relative error of at most 0.0003.
Values sent between devices are 32-bit elements; how exact they have to be, the bound alone decides.
No kernel may reach another device: no remote copies, remote signals or barrier semaphores. Data moves between devices by JAX's collectives and lax.ppermute only.
A program may use at most 64 MiB of HBM per device.

v0:
```python
import jax
import jax.numpy as jnp
from jax import lax
from jax.sharding import PartitionSpec as P

STEPS = 2
TAYLOR = 4
spacing = 0.5
time_step = 0.04
highest = lax.Precision.HIGHEST


def extended_2(block, sides, width):
    for axis, dim in sides:
        count = lax.axis_size(axis)
        forward = [(i, i + 1) for i in range(count - 1)]
        backward = [(target, source) for source, target in forward]
        low = lax.ppermute(
            lax.slice_in_dim(block, block.shape[dim] - width, None, axis=dim), axis, forward
        )
        high = lax.ppermute(lax.slice_in_dim(block, 0, width, axis=dim), axis, backward)
        block = jnp.concatenate([low, block, high], axis=dim)
    return block


def laplace(extended):
    middle = extended[:, :, 2:-2]
    along_z = 16.0 * (extended[:, :, 3:-1] + extended[:, :, 1:-3]) - (
        extended[:, :, 4:] + extended[:, :, :-4]
    )
    along_x = 16.0 * (jnp.roll(middle, 1, 3) + jnp.roll(middle, -1, 3)) - (
        jnp.roll(middle, 2, 3) + jnp.roll(middle, -2, 3)
    )
    along_y = 16.0 * (jnp.roll(middle, 1, 4) + jnp.roll(middle, -1, 4)) - (
        jnp.roll(middle, 2, 4) + jnp.roll(middle, -2, 4)
    )
    return (along_z + along_x + along_y - 90.0 * middle) / (12.0 * spacing * spacing)


def projections(ace_rows, term):
    vector_count = ace_rows.shape[0]
    orbital_count = term.shape[0]
    products = lax.dot_general(
        ace_rows.reshape(vector_count * 2, -1),
        term.reshape(orbital_count * 2, -1),
        (((1,), (1,)), ((), ())),
        precision=highest,
        preferred_element_type=jnp.float32,
    )
    products = products.reshape(vector_count, 2, orbital_count, 2)
    return jnp.stack(
        [products[:, 0, :, 0] + products[:, 1, :, 1], products[:, 0, :, 1] - products[:, 1, :, 0]]
    )


def ace_weights(ace_rows, term):
    return lax.psum(projections(ace_rows, term), "dom")


def fock_term(ace_rows, weights):
    vector_count = ace_rows.shape[0]
    orbital_count = weights.shape[2]
    real_part = weights[0]
    imag_part = weights[1]
    coefficients = jnp.stack(
        [jnp.stack([real_part, imag_part], axis=-1), jnp.stack([-imag_part, real_part], axis=-1)],
        axis=1,
    )
    applied = lax.dot_general(
        coefficients.reshape(vector_count * 2, orbital_count * 2),
        ace_rows.reshape(vector_count * 2, -1),
        (((0,), (0,)), ((), ())),
        precision=highest,
        preferred_element_type=jnp.float32,
    )
    return applied.reshape((orbital_count, 2) + ace_rows.shape[2:])


def next_term(applied, degree):
    factor = time_step / degree
    return jnp.stack([factor * applied[:, 1], -factor * applied[:, 0]], axis=1)


def taylor_rounds(current, potential, ace_vectors):
    accumulated = current
    term = current
    for degree in range(1, TAYLOR + 1):
        extended = extended_2(term, (("dom", 2),), 2)
        weights = ace_weights(ace_vectors, term)
        applied = -0.5 * laplace(extended) + potential * term - fock_term(ace_vectors, weights)
        term = next_term(applied, degree)
        accumulated = accumulated + term
    return accumulated


def atom_partials(current, run_projectors, run_atom, run_count, run_start, kb_energy):
    row_count = current.shape[0] * 2
    point_count = run_projectors.shape[2]
    atom_dev = kb_energy.shape[0]
    dom_count = lax.axis_size("dom")
    slot_count = run_atom.shape[0]
    flattened = current.reshape(row_count, -1)

    def cut_run(run_begin):
        return lax.dynamic_slice_in_dim(flattened, run_begin, point_count, 1)

    pieces = jax.vmap(cut_run)(run_start)
    in_run = jnp.arange(point_count, dtype=jnp.int32)[None, :] < run_count[:, None]
    masked = jnp.where(in_run[:, None, :], run_projectors, 0.0)
    partials = jnp.einsum("scp,srp->scr", masked, pieces, precision=highest)
    capacity = 2 * slot_count // dom_count
    owner = run_atom // atom_dev
    slot_ids = jnp.arange(slot_count, dtype=jnp.int32)
    same_owner = (owner[:, None] == owner[None, :]) & (slot_ids[None, :] < slot_ids[:, None])
    owner_rank = jnp.sum(same_owner.astype(jnp.int32), axis=1)
    slot_pos = owner * capacity + owner_rank
    placement = jnp.arange(dom_count * capacity, dtype=jnp.int32)[:, None] == slot_pos[None, :]
    outgoing = jnp.einsum("ks,scr->kcr", placement.astype(jnp.float32), partials, precision=highest)
    atom_slots = jnp.max(jnp.where(placement, (run_atom % atom_dev)[None, :], -1), axis=1)
    received, received_ids = (
        lax.all_to_all(outgoing, "dom", split_axis=0, concat_axis=0, tiled=True),
        lax.all_to_all(atom_slots, "dom", split_axis=0, concat_axis=0, tiled=True),
    )
    matches = (received_ids[None, :] == jnp.arange(atom_dev, dtype=jnp.int32)[:, None]).astype(
        jnp.float32
    )
    atom_totals = jnp.einsum("ak,kcr->acr", matches, received, precision=highest)
    return (
        2.0
        * kb_energy[None, :]
        * jnp.einsum("ar,acr->ca", atom_totals[:, 0], atom_totals[:, 1:], precision=highest)
    )


def shards(
    orbitals,
    ace_vectors,
    local_potential,
    field_strength,
    run_projectors,
    run_atom,
    run_count,
    run_start,
    kb_energy,
):
    plane_count = orbitals.shape[2]
    plane_total = plane_count * lax.axis_size("dom")
    first_plane = lax.axis_index("dom") * plane_count
    height = (
        2.0
        * ((first_plane + jnp.arange(plane_count, dtype=jnp.int32)).astype(jnp.float32) + 0.5)
        / plane_total
        - 1.0
    )
    current = orbitals
    results = []
    for step_index in range(STEPS):
        strength = field_strength[step_index]
        current = taylor_rounds(
            current, local_potential + strength * height[:, None, None], ace_vectors
        )
        partial_force = atom_partials(
            current, run_projectors, run_atom, run_count, run_start, kb_energy
        )
        partial_force = lax.psum(partial_force, "band")
        results.append(partial_force)
    forces = jnp.stack(results)
    return (current, forces)


def solution(mesh):
    in_specs = (
        P("band", None, "dom", None, None),
        P(None, None, "dom", None, None),
        P("dom", None, None),
        P(),
        P("dom", None, None),
        P("dom"),
        P("dom"),
        P("dom"),
        P("dom"),
    )
    out_specs = (P("band", None, "dom", None, None), P(None, None, "dom"))
    return jax.shard_map(shards, mesh=mesh, in_specs=in_specs, out_specs=out_specs, check_vma=False)
```

profile of v0, /device:TPU:1, one launch (start us, length us, event | category | flops | bytes accessed | tf_op | source)
XLA Modules:
  0.0 938.4 jit_solution(7851821572021941752)
XLA Ops:
  2.0 4.5 collective-permute-start.1
  7.2 1.3 collective-permute-start
  10.0 14.1 %all-to-all-start = ((s32[32,2,1]{1,2,0:T(1,128)}), s32[32,2,1]{1,2,0:T(1,128)}, u32[]{:S(2)}, u32[]{:S(2)}) async-start(s32[32,2,1]{1,2,0:T(1,128)} %bitcast.89), calls=%async_computation | async-start | bytes 32768 | tf_op jit(solution)/shard_map/all_to_all | solution.py:122
  24.2 5.0 convolution_bitcast_fusion
  29.2 60.4 %psum.70 = f32[2,16,2]{1,2,0:T(2,128)S(1)} all-reduce(f32[2,16,2]{1,2,0:T(2,128)S(1)} %pad_maximum_fusion.23), channel_id=1, replica_groups=mesh['band'=16,'dom'=32] {'dom'}, use_global_device_ids=true, to_apply=%region_0.0 | all-reduce | flops 64 | bytes 512 | tf_op jit(solution)/shard_map/psum | solution.py:57
  96.3 1.2 broadcast_multiply_fusion.1
  111.2 1.4 reduce.31
  115.1 2.7 convolution_subtract_fusion.7
  118.2 0.9 convolution_bitcast_fusion.7
  119.4 55.7 %psum.71 = f32[2,16,2]{1,2,0:T(2,128)S(1)} all-reduce(f32[2,16,2]{1,2,0:T(2,128)S(1)} %pad_maximum_fusion.26), channel_id=1, replica_groups=mesh['band'=16,'dom'=32] {'dom'}, use_global_device_ids=true, to_apply=%region_1.2 | all-reduce | flops 64 | bytes 512 | tf_op jit(solution)/shard_map/psum | solution.py:57
  180.3 1.5 collective-permute-start.2
  181.8 4.6 collective-permute-start.3
  187.1 1.0 pad_maximum_fusion
  188.8 2.0 convolution_subtract_fusion.6
  191.2 0.9 convolution_bitcast_fusion.6
  192.4 57.9 %psum.72 = f32[2,16,2]{1,2,0:T(2,128)S(1)} all-reduce(f32[2,16,2]{1,2,0:T(2,128)S(1)} %pad_maximum_fusion.29), channel_id=1, replica_groups=mesh['band'=16,'dom'=32] {'dom'}, use_global_device_ids=true, to_apply=%region_2.3 | all-reduce | flops 64 | bytes 512 | tf_op jit(solution)/shard_map/psum | solution.py:57
  251.1 1.0 fusion.49
  256.1 1.3 collective-permute-start.4
  257.4 4.6 collective-permute-start.5
  262.7 0.9 pad_maximum_fusion.1
  263.7 2.8 convolution_subtract_fusion.5
  266.9 0.9 convolution_bitcast_fusion.5
  268.1 57.5 %psum.73 = f32[2,16,2]{1,2,0:T(2,128)S(1)} all-reduce(f32[2,16,2]{1,2,0:T(2,128)S(1)} %pad_maximum_fusion.32), channel_id=1, replica_groups=mesh['band'=16,'dom'=32] {'dom'}, use_global_device_ids=true, to_apply=%region_3.4 | all-reduce | flops 64 | bytes 512 | tf_op jit(solution)/shard_map/psum | solution.py:57
  326.4 1.0 fusion.41
  327.5 1.1 fusion.42
  331.5 1.3 collective-permute-start.6
  332.8 4.8 collective-permute-start.7
  338.1 0.9 pad_maximum_fusion.2
  339.8 2.9 convolution_subtract_fusion.4
  343.5 0.9 convolution_bitcast_fusion.4
  344.7 57.5 %psum.74 = f32[2,16,2]{1,2,0:T(2,128)S(1)} all-reduce(f32[2,16,2]{1,2,0:T(2,128)S(1)} %pad_maximum_fusion.35), channel_id=1, replica_groups=mesh['band'=16,'dom'=32] {'dom'}, use_global_device_ids=true, to_apply=%region_4.5 | all-reduce | flops 64 | bytes 512 | tf_op jit(solution)/shard_map/psum | solution.py:57
  408.9 43.4 %while.2 = (s32[]{:T(128)}, f32[4,8192]{1,0:T(4,128)S(1)}, s32[32,2]{0,1:T(2,128)S(1)}, f32[32,4,256]{2,1,0:T(4,128)S(1)}, s32[]{:T(128)}) while((s32[]{:T(128)}, f32[4,8192]{1,0:T(4,128)S(1)}, s32[32,2]{0,1:T(2,128)S(1)}, f32[32,4,256]{2,1,0:T(4,128)S(1)}, s32[]{:T(128)}) %tuple.152), condition=%wide.while_cond, body=%wide.while_body.sunk | while | flops 2 | bytes 8297 | solution.py:105
  454.4 16.1 %all-to-all-start.1 = ((f32[64,4,4]{2,1,0:T(4,128)}), f32[64,4,4]{2,1,0:T(4,128)S(1)}, u32[]{:S(2)}, u32[]{:S(2)}) async-start(f32[64,4,4]{2,1,0:T(4,128)} %copy.269), calls=%async_computation.1 | async-start | bytes 262144 | tf_op jit(solution)/shard_map/all_to_all | solution.py:121
  471.4 3.9 collective-permute-start.9
  475.3 1.3 collective-permute-start.8
  476.6 3.2 all-to-all-done.1
  481.9 3.3 convolution_subtract_fusion.3
  485.6 0.9 convolution_bitcast_fusion.3
  486.8 58.0 %psum.75 = f32[2,16,2]{1,2,0:T(2,128)S(1)} all-reduce(f32[2,16,2]{1,2,0:T(2,128)S(1)} %pad_maximum_fusion.38), channel_id=1, replica_groups=mesh['band'=16,'dom'=32] {'dom'}, use_global_device_ids=true, to_apply=%region_5.6 | all-reduce | flops 64 | bytes 512 | tf_op jit(solution)/shard_map/psum | solution.py:57
  544.8 1.1 fusion.37
  545.9 1.1 fusion.38
  551.4 1.3 collective-permute-start.10
  552.7 5.0 collective-permute-start.11
  559.3 1.0 pad_maximum_fusion.3
  561.1 3.1 convolution_subtract_fusion.2
  565.8 56.2 %psum.76 = f32[2,16,2]{1,2,0:T(2,128)S(1)} all-reduce(f32[2,16,2]{1,2,0:T(2,128)S(1)} %pad_maximum_fusion.41), channel_id=1, replica_groups=mesh['band'=16,'dom'=32] {'dom'}, use_global_device_ids=true, to_apply=%region_6.7 | all-reduce | flops 64 | bytes 512 | tf_op jit(solution)/shard_map/psum | solution.py:57
  622.0 1.0 fusion.29
  623.1 1.1 fusion.30
  624.5 1.1 fusion.26
  629.3 1.3 collective-permute-start.12
  630.6 4.6 collective-permute-start.13
  636.8 1.0 pad_maximum_fusion.4
  638.6 3.2 convolution_subtract_fusion.1
  642.1 0.9 convolution_bitcast_fusion.1
  643.3 56.6 %psum.77 = f32[2,16,2]{1,2,0:T(2,128)S(1)} all-reduce(f32[2,16,2]{1,2,0:T(2,128)S(1)} %pad_maximum_fusion.44), channel_id=1, replica_groups=mesh['band'=16,'dom'=32] {'dom'}, use_global_device_ids=true, to_apply=%region_7.8 | all-reduce | flops 64 | bytes 512 | tf_op jit(solution)/shard_map/psum | solution.py:57
  704.5 1.3 collective-permute-start.14
  705.8 4.7 collective-permute-start.15
  711.1 1.0 pad_maximum_fusion.5
  712.8 2.0 convolution_subtract_fusion
  715.0 0.9 maximum_add_fusion.33
  716.6 39.1 %while.3 = (s32[]{:T(128)}, f32[4,8192]{1,0:T(4,128)S(1)}, s32[32,2]{0,1:T(2,128)S(1)}, f32[32,4,256]{2,1,0:T(4,128)S(1)}, s32[]{:T(128)}) while((s32[]{:T(128)}, f32[4,8192]{1,0:T(4,128)S(1)}, s32[32,2]{0,1:T(2,128)S(1)}, f32[32,4,256]{2,1,0:T(4,128)S(1)}, s32[]{:T(128)}) %tuple.158), condition=%wide.while_cond.1, body=%wide.while_body.1.sunk | while | flops 2 | bytes 8297 | solution.py:105
  757.8 20.5 %all-to-all-start.2 = ((f32[64,4,4]{2,1,0:T(4,128)}), f32[64,4,4]{2,1,0:T(4,128)S(1)}, u32[]{:S(2)}, u32[]{:S(2)}) async-start(f32[64,4,4]{2,1,0:T(4,128)} %copy.273), calls=%async_computation.2 | async-start | bytes 262144 | tf_op jit(solution)/shard_map/all_to_all | solution.py:121
  778.6 9.1 all-to-all-done.2
  788.7 149.0 %all-reduce.1 = (f32[1,3,4]{2,1,0:T(4,128)S(1)}, f32[1,3,4]{2,1,0:T(4,128)S(1)}) all-reduce(f32[1,3,4]{2,1,0:T(4,128)S(1)} %get-tuple-element.269, f32[1,3,4]{2,1,0:T(4,128)S(1)} %get-tuple-element.268), channel_id=1, replica_groups=mesh['band'=16,'dom'=32] {'band'}, use_global_device_ids=true, to_apply=%region_11.12 | all-reduce | flops 24 | bytes 192 | tf_op jit(solution)/shard_map/psum | solution.py:165
  (605 shorter events, 166.3 us)
Async XLA Ops:
  1.4 22.7 %copy-start = (f32[2,2,8,8,128]{4,3,2,1,0:T(8,128)S(1)}, f32[2,2,8,8,128]{4,3,2,1,0:T(8,128)}, u32[]{:S(2)}) copy-start(f32[2,2,8,8,128]{4,3,2,1,0:T(8,128)} %param.9) | copy-start | bytes 393220
  2.0 111.2 %collective-permute-start.1 = (f32[2,2,2,8,128]{4,1,3,2,0:T(2,128)}, f32[2,2,2,8,128]{4,1,3,2,0:T(2,128)}, u32[]{:S(2)}, u32[]{:S(2)}) collective-permute-start(f32[2,2,2,8,128]{4,1,3,2,0:T(2,128)} %copy.378), channel_id=1, source_target_pairs={{0,1},{1,2},{2,3},{3,4},{4,5},{5,6},{6,7},{7,8},{8,9},{9,10},{10,1... | collective-permute-start | bytes 98312 | tf_op jit(solution)/shard_map/ppermute | solution.py:18
  6.6 1.9 copy-start.71
  7.2 107.0 %collective-permute-start = (f32[2,2,2,8,128]{4,1,3,2,0:T(2,128)}, f32[2,2,2,8,128]{4,1,3,2,0:T(2,128)}, u32[]{:S(2)}, u32[]{:S(2)}) collective-permute-start(f32[2,2,2,8,128]{4,1,3,2,0:T(2,128)} %copy.379), channel_id=1, source_target_pairs={{1,0},{2,1},{3,2},{4,3},{5,4},{6,5},{7,6},{8,7},{9,8},{10,9},{11,1... | collective-permute-start | bytes 98312 | tf_op jit(solution)/shard_map/ppermute | solution.py:21
  10.0 100.7 %all-to-all-start = ((s32[32,2,1]{1,2,0:T(1,128)}), s32[32,2,1]{1,2,0:T(1,128)}, u32[]{:S(2)}, u32[]{:S(2)}) async-start(s32[32,2,1]{1,2,0:T(1,128)} %bitcast.89), calls=%async_computation | async-start | bytes 32768 | tf_op jit(solution)/shard_map/all_to_all | solution.py:122
  91.7 6.5 copy-start.1
  93.8 1.3 copy-start.72
  93.8 1.9 copy-start.68
  93.8 1.9 copy-start.73
  94.5 3.0 copy-start.44
  106.3 2.1 copy-start.11
  113.3 1.8 copy-start.52
  113.3 1.8 copy-start.53
  114.1 1.0 copy-start.33
  114.1 1.1 copy-start.34
  180.3 6.3 collective-permute-start.2
  181.8 5.3 collective-permute-start.3
  186.6 1.5 copy-start.28
  186.6 1.5 copy-start.29
  186.6 1.5 copy-start.38
  186.6 1.5 copy-start.39
  187.1 1.0 copy-start.57
  187.1 1.0 copy-start.58
  187.1 1.0 copy-start.61
  256.1 6.1 collective-permute-start.4
  257.4 5.3 collective-permute-start.5
  262.2 1.5 copy-start.20
  262.2 1.5 copy-start.30
  262.2 1.5 copy-start.31
  262.2 1.5 copy-start.40
  262.3 1.5 copy-start.41
  331.5 6.3 collective-permute-start.6
  332.8 5.3 collective-permute-start.7
  337.8 1.3 copy-start.15
  337.8 1.3 copy-start.21
  337.8 1.3 copy-start.22
  337.8 1.3 copy-start.37
  408.8 43.5 %copy-start.9 = (f32[32,4,256]{2,1,0:T(4,128)S(1)}, f32[32,4,256]{2,1,0:T(4,128)}, u32[]{:S(2)}) copy-start(f32[32,4,256]{2,1,0:T(4,128)} %param.13) | copy-start | bytes 393220
  454.4 25.4 %all-to-all-start.1 = ((f32[64,4,4]{2,1,0:T(4,128)}), f32[64,4,4]{2,1,0:T(4,128)S(1)}, u32[]{:S(2)}, u32[]{:S(2)}) async-start(f32[64,4,4]{2,1,0:T(4,128)} %copy.269), calls=%async_computation.1 | async-start | bytes 262144 | tf_op jit(solution)/shard_map/all_to_all | solution.py:121
  471.4 9.8 %copy-start.27 = (f32[2,2,8,8,126]{4,1,3,2,0:T(2,128)S(1)}, f32[2,2,8,8,126]{4,1,3,2,0:T(2,128)}, u32[]{:S(2)}) copy-start(f32[2,2,8,8,126]{4,1,3,2,0:T(2,128)} %get-tuple-element.142) | copy-start | bytes 387076
  471.4 9.8 %collective-permute-start.9 = (f32[2,2,2,8,128]{4,1,3,2,0:T(2,128)}, f32[2,2,2,8,128]{4,1,3,2,0:T(2,128)}, u32[]{:S(2)}, u32[]{:S(2)}) collective-permute-start(f32[2,2,2,8,128]{4,1,3,2,0:T(2,128)} %get-tuple-element.127), channel_id=1, source_target_pairs={{0,1},{1,2},{2,3},{3,4},{4,5},{5,6},{6,7},{7,8},{8,9},{9,10},{10,1... | collective-permute-start | bytes 98312 | tf_op jit(solution)/shard_map/ppermute | solution.py:18
  475.3 5.9 collective-permute-start.8
  551.4 7.9 collective-permute-start.10
  552.7 6.6 collective-permute-start.11
  559.3 1.1 copy-start.12
  559.3 1.1 copy-start.13
  559.3 1.1 copy-start.16
  559.3 1.1 copy-start.17
  629.3 7.5 collective-permute-start.12
  630.6 6.2 collective-permute-start.13
  636.7 1.1 copy-start.14
  636.7 1.1 copy-start.18
  636.7 1.1 copy-start.19
  636.7 1.1 copy-start.23
  704.5 6.3 collective-permute-start.14
  705.8 5.3 collective-permute-start.15
  710.7 1.3 copy-start.35
  710.8 1.3 copy-start.36
  711.1 1.0 copy-start.59
  711.1 1.0 copy-start.60
  757.8 20.5 %slice-start = ((f32[4,4,4]{2,0,1:T(4,128)}), f32[4,3,4]{2,0,1:T(4,128)S(1)}, s32[]{:S(2)}) async-start(f32[4,4,4]{2,0,1:T(4,128)} %copy-done.51), calls=%async_computation.3 | async-start | bytes 12288 | tf_op jit(solution)/shard_map/slice | solution.py:131
  757.8 20.5 %copy-start.66 = (f32[4,1,4]{2,0,1:T(4,128)S(1)}, f32[4,1,4]{2,0,1:T(4,128)}, u32[]{:S(2)}) copy-start(f32[4,1,4]{2,0,1:T(4,128)} %slice.1403) | copy-start | bytes 196
  757.8 29.9 %all-to-all-start.2 = ((f32[64,4,4]{2,1,0:T(4,128)}), f32[64,4,4]{2,1,0:T(4,128)S(1)}, u32[]{:S(2)}, u32[]{:S(2)}) async-start(f32[64,4,4]{2,1,0:T(4,128)} %copy.273), calls=%async_computation.2 | async-start | bytes 262144 | tf_op jit(solution)/shard_map/all_to_all | solution.py:121
  778.5 9.2 copy-start.65
  (33 other events, 26.2 us)
where the time goes:
time: 950 us; the launch traced here: 938 us
  blocking collectives  609 us (64%)
  local copies, waits for them, and re-layouts  129 us (14%)
  starting transfers between devices  97.9 us (10%)
  other arithmetic  50.1 us (5%)
  matrix products  36 us (4%)
  waiting for transfers between devices  13.9 us (1%)
    psum x8, blocking collectives, ace_weights(): return lax.psum(projections(ace_rows, term), 'dom')  460 us
    psum x1, blocking collectives, shards(): partial_force = lax.psum(partial_force, 'band')  149 us
    gather x192, local copies, waits for them, and re-layouts  82.4 us
    ppermute x8, starting transfers between devices, extended_2(): lax.ppermute(lax.slice_in_dim(block, block.shape[dim] - width, None, axis...  36.6 us
    all_to_all x2, starting transfers between devices, atom_partials(): lax.all_to_all(outgoing, 'dom', split_axis=0, concat_axis=0, tiled=True)  36.6 us
    another operation x60, other arithmetic, next_term(): return jnp.stack([factor * applied[:, 1], -factor * applied[:, 0]], axis=1)  35.7 us
    unnamed x177, local copies, waits for them, and re-layouts  22.7 us
    dot_general x8, matrix products, fock_term(): lax.dot_general(coefficients.reshape(vector_count * 2, orbital_count * 2)...  22.2 us
  transfers between devices with their start and end apart: 19, of which 6 were waited for; matrix products, arithmetic and copies ran while one was open for 3% of the time, Pallas kernels for 0%

commit v1 on v0

--- a/solution.py
+++ b/solution.py
@@ -54,7 +54,7 @@
 
 
 def ace_weights(ace_rows, term):
-    return lax.psum(projections(ace_rows, term), "dom")
+    return jnp.sum(lax.all_gather(projections(ace_rows, term), "dom"), axis=0)
 
 
 def fock_term(ace_rows, weights):

time: 950 us -> 765 us (0.81)
  blocking collectives: 609 us -> 442 us
  starting transfers between devices: 97.9 us -> 79.5 us
    psum x8 -> x0, blocking collectives: 460 us -> none  [ace_weights(): return lax.psum(projections(ace_rows, term), 'dom')]
    all_gather x0 -> x8, blocking collectives: none -> 309 us  [ace_weights(): return jnp.sum(lax.all_gather(projections(ace_rows, term), 'dom'), axis=0)]
    all_to_all x2, starting transfers between devices: 36.6 us -> 18.6 us  [atom_partials(): lax.all_to_all(outgoing, 'dom', split_axis=0, concat_axis=0, tiled=True)]
    psum x1, blocking collectives: 149 us -> 133 us  [shards(): partial_force = lax.psum(partial_force, 'band')]
  transfers between devices with their start and end apart: 19 -> 19, of which waited for: 6 -> 6; matrix products, arithmetic and copies ran while one was open for 3% -> 4% of each run, Pallas kernels for 0% -> 0%
where the time goes in v1:
time: 765 us; the launch traced here: 754 us
  blocking collectives  442 us (58%)
  local copies, waits for them, and re-layouts  129 us (17%)
  starting transfers between devices  79.5 us (10%)
  other arithmetic  50.6 us (7%)
  matrix products  36 us (5%)
  waiting for transfers between devices  14.2 us (2%)
    all_gather x8, blocking collectives, ace_weights(): return jnp.sum(lax.all_gather(projections(ace_rows, term), 'dom'), axis=0)  309 us
    psum x1, blocking collectives, shards(): partial_force = lax.psum(partial_force, 'band')  133 us
    gather x192, local copies, waits for them, and re-layouts  82.4 us
    ppermute x8, starting transfers between devices, extended_2(): lax.ppermute(lax.slice_in_dim(block, block.shape[dim] - width, None, axis...  36.1 us
    another operation x60, other arithmetic, next_term(): return jnp.stack([factor * applied[:, 1], -factor * applied[:, 0]], axis=1)  35.7 us
    unnamed x177, local copies, waits for them, and re-layouts  22.7 us
    dot_general x8, matrix products, fock_term(): lax.dot_general(coefficients.reshape(vector_count * 2, orbital_count * 2)...  22.2 us
    all_to_all x2, starting transfers between devices, atom_partials(): lax.all_to_all(outgoing, 'dom', split_axis=0, concat_axis=0, tiled=True)  18.6 us
  transfers between devices with their start and end apart: 19, of which 6 were waited for; matrix products, arithmetic and copies ran while one was open for 4% of the time, Pallas kernels for 0%

profile of v1, /device:TPU:1, one launch (start us, length us, event | category | flops | bytes accessed | tf_op | source)
XLA Modules:
  0.0 754.5 jit_solution(955985360155348435)
XLA Ops:
  2.0 4.5 collective-permute-start.1
  7.2 1.3 collective-permute-start
  10.0 14.1 %all-to-all-start = ((s32[32,2,1]{1,2,0:T(1,128)}), s32[32,2,1]{1,2,0:T(1,128)}, u32[]{:S(2)}, u32[]{:S(2)}) async-start(s32[32,2,1]{1,2,0:T(1,128)} %bitcast.97), calls=%async_computation | async-start | bytes 32768 | tf_op jit(solution)/shard_map/all_to_all | solution.py:122
  24.2 5.0 convolution_bitcast_fusion
  29.2 37.1 %all-gather = f32[64,16,2]{1,2,0:T(2,128)S(1)} all-gather(f32[2,16,2]{1,2,0:T(2,128)S(1)} %pad_maximum_fusion.23), channel_id=2, replica_groups=mesh['band'=16,'dom'=32] {'dom'}, dimensions={0}, use_global_device_ids=true | all-gather | bytes 8448 | tf_op jit(solution)/shard_map/all_gather | solution.py:57
  73.0 1.2 broadcast_multiply_fusion.1
  88.0 1.4 reduce.31
  91.9 2.7 convolution_subtract_fusion.7
  95.0 0.9 convolution_bitcast_fusion.7
  96.2 35.4 %all-gather.1 = f32[64,16,2]{1,2,0:T(2,128)S(1)} all-gather(f32[2,16,2]{1,2,0:T(2,128)S(1)} %pad_maximum_fusion.26), channel_id=3, replica_groups=mesh['band'=16,'dom'=32] {'dom'}, dimensions={0}, use_global_device_ids=true | all-gather | bytes 8448 | tf_op jit(solution)/shard_map/all_gather | solution.py:57
  136.8 1.3 collective-permute-start.2
  138.1 4.6 collective-permute-start.3
  143.4 1.0 pad_maximum_fusion
  145.1 2.0 convolution_subtract_fusion.6
  147.5 0.9 convolution_bitcast_fusion.6
  148.7 38.9 %all-gather.2 = f32[64,16,2]{1,2,0:T(2,128)S(1)} all-gather(f32[2,16,2]{1,2,0:T(2,128)S(1)} %pad_maximum_fusion.29), channel_id=4, replica_groups=mesh['band'=16,'dom'=32] {'dom'}, dimensions={0}, use_global_device_ids=true | all-gather | bytes 8448 | tf_op jit(solution)/shard_map/all_gather | solution.py:57
  188.4 1.0 fusion.49
  193.5 1.3 collective-permute-start.4
  194.8 4.6 collective-permute-start.5
  200.1 0.9 pad_maximum_fusion.1
  201.1 2.8 convolution_subtract_fusion.5
  204.3 0.9 convolution_bitcast_fusion.5
  205.5 41.6 %all-gather.3 = f32[64,16,2]{1,2,0:T(2,128)S(1)} all-gather(f32[2,16,2]{1,2,0:T(2,128)S(1)} %pad_maximum_fusion.32), channel_id=5, replica_groups=mesh['band'=16,'dom'=32] {'dom'}, dimensions={0}, use_global_device_ids=true | all-gather | bytes 8448 | tf_op jit(solution)/shard_map/all_gather | solution.py:57
  247.9 1.0 fusion.41
  249.0 1.1 fusion.42
  253.0 1.3 collective-permute-start.6
  254.3 4.6 collective-permute-start.7
  259.6 0.9 pad_maximum_fusion.2
  261.3 2.9 convolution_subtract_fusion.4
  265.0 0.9 convolution_bitcast_fusion.4
  266.2 39.6 %all-gather.4 = f32[64,16,2]{1,2,0:T(2,128)S(1)} all-gather(f32[2,16,2]{1,2,0:T(2,128)S(1)} %pad_maximum_fusion.35), channel_id=6, replica_groups=mesh['band'=16,'dom'=32] {'dom'}, dimensions={0}, use_global_device_ids=true | all-gather | bytes 8448 | tf_op jit(solution)/shard_map/all_gather | solution.py:57
  312.5 43.4 %while.2 = (s32[]{:T(128)}, f32[4,8192]{1,0:T(4,128)S(1)}, s32[32,2]{0,1:T(2,128)S(1)}, f32[32,4,256]{2,1,0:T(4,128)S(1)}, s32[]{:T(128)}) while((s32[]{:T(128)}, f32[4,8192]{1,0:T(4,128)S(1)}, s32[32,2]{0,1:T(2,128)S(1)}, f32[32,4,256]{2,1,0:T(4,128)S(1)}, s32[]{:T(128)}) %tuple.152), condition=%wide.while_cond, body=%wide.while_body.sunk | while | flops 2 | bytes 8297 | solution.py:105
  358.0 7.4 all-to-all-start.1
  366.3 3.9 collective-permute-start.9
  370.2 1.7 collective-permute-start.8
  371.9 3.0 all-to-all-done.1
  377.1 3.3 convolution_subtract_fusion.3
  380.8 0.9 convolution_bitcast_fusion.3
  382.0 36.9 %all-gather.5 = f32[64,16,2]{1,2,0:T(2,128)S(1)} all-gather(f32[2,16,2]{1,2,0:T(2,128)S(1)} %pad_maximum_fusion.38), channel_id=7, replica_groups=mesh['band'=16,'dom'=32] {'dom'}, dimensions={0}, use_global_device_ids=true | all-gather | bytes 8448 | tf_op jit(solution)/shard_map/all_gather | solution.py:57
  418.9 1.1 fusion.37
  420.0 1.1 fusion.38
  425.5 1.3 collective-permute-start.10
  426.8 4.6 collective-permute-start.11
  433.0 1.0 pad_maximum_fusion.3
  434.8 3.1 convolution_subtract_fusion.2
  439.5 40.4 %all-gather.6 = f32[64,16,2]{1,2,0:T(2,128)S(1)} all-gather(f32[2,16,2]{1,2,0:T(2,128)S(1)} %pad_maximum_fusion.41), channel_id=8, replica_groups=mesh['band'=16,'dom'=32] {'dom'}, dimensions={0}, use_global_device_ids=true | all-gather | bytes 8448 | tf_op jit(solution)/shard_map/all_gather | solution.py:57
  480.0 1.0 fusion.29
  481.0 1.1 fusion.30
  482.5 1.1 fusion.26
  487.2 1.3 collective-permute-start.12
  488.5 4.7 collective-permute-start.13
  494.9 1.0 pad_maximum_fusion.4
  496.7 3.2 convolution_subtract_fusion.1
  500.2 0.9 convolution_bitcast_fusion.1
  501.4 39.3 %all-gather.7 = f32[64,16,2]{1,2,0:T(2,128)S(1)} all-gather(f32[2,16,2]{1,2,0:T(2,128)S(1)} %pad_maximum_fusion.44), channel_id=9, replica_groups=mesh['band'=16,'dom'=32] {'dom'}, dimensions={0}, use_global_device_ids=true | all-gather | bytes 8448 | tf_op jit(solution)/shard_map/all_gather | solution.py:57
  545.3 1.3 collective-permute-start.14
  546.6 4.6 collective-permute-start.15
  551.9 1.0 pad_maximum_fusion.5
  553.6 2.0 convolution_subtract_fusion
  555.8 0.9 maximum_add_fusion.33
  557.4 39.1 %while.3 = (s32[]{:T(128)}, f32[4,8192]{1,0:T(4,128)S(1)}, s32[32,2]{0,1:T(2,128)S(1)}, f32[32,4,256]{2,1,0:T(4,128)S(1)}, s32[]{:T(128)}) while((s32[]{:T(128)}, f32[4,8192]{1,0:T(4,128)S(1)}, s32[32,2]{0,1:T(2,128)S(1)}, f32[32,4,256]{2,1,0:T(4,128)S(1)}, s32[]{:T(128)}) %tuple.158), condition=%wide.while_cond.1, body=%wide.while_body.1.sunk | while | flops 2 | bytes 8297 | solution.py:105
  598.6 11.2 %all-to-all-start.2 = ((f32[64,4,4]{2,1,0:T(4,128)}), f32[64,4,4]{2,1,0:T(4,128)S(1)}, u32[]{:S(2)}, u32[]{:S(2)}) async-start(f32[64,4,4]{2,1,0:T(4,128)} %copy.273), calls=%async_computation.2 | async-start | bytes 262144 | tf_op jit(solution)/shard_map/all_to_all | solution.py:121
  610.0 9.2 %all-to-all-done.2 = f32[64,4,4]{2,1,0:T(4,128)S(1)} async-done(((f32[64,4,4]{2,1,0:T(4,128)}), f32[64,4,4]{2,1,0:T(4,128)S(1)}, u32[]{:S(2)}, u32[]{:S(2)}) %all-to-all-start.2) | async-done | bytes 4128 | tf_op jit(solution)/shard_map/all_to_all | solution.py:121
  620.2 133.5 %all-reduce.1 = (f32[1,3,4]{2,1,0:T(4,128)S(1)}, f32[1,3,4]{2,1,0:T(4,128)S(1)}) all-reduce(f32[1,3,4]{2,1,0:T(4,128)S(1)} %get-tuple-element.269, f32[1,3,4]{2,1,0:T(4,128)S(1)} %get-tuple-element.268), channel_id=1, replica_groups=mesh['band'=16,'dom'=32] {'band'}, use_global_device_ids=true, to_apply=%region_11.12 | all-reduce | flops 24 | bytes 192 | tf_op jit(solution)/shard_map/psum | solution.py:165
  (613 shorter events, 167.1 us)
Async XLA Ops:
  1.4 22.7 %copy-start = (f32[2,2,8,8,128]{4,3,2,1,0:T(8,128)S(1)}, f32[2,2,8,8,128]{4,3,2,1,0:T(8,128)}, u32[]{:S(2)}) copy-start(f32[2,2,8,8,128]{4,3,2,1,0:T(8,128)} %param.9) | copy-start | bytes 393220
  2.0 88.0 %collective-permute-start.1 = (f32[2,2,2,8,128]{4,1,3,2,0:T(2,128)}, f32[2,2,2,8,128]{4,1,3,2,0:T(2,128)}, u32[]{:S(2)}, u32[]{:S(2)}) collective-permute-start(f32[2,2,2,8,128]{4,1,3,2,0:T(2,128)} %copy.378), channel_id=1, source_target_pairs={{0,1},{1,2},{2,3},{3,4},{4,5},{5,6},{6,7},{7,8},{8,9},{9,10},{10,1... | collective-permute-start | bytes 98312 | tf_op jit(solution)/shard_map/ppermute | solution.py:18
  6.6 1.9 copy-start.71
  7.2 83.8 %collective-permute-start = (f32[2,2,2,8,128]{4,1,3,2,0:T(2,128)}, f32[2,2,2,8,128]{4,1,3,2,0:T(2,128)}, u32[]{:S(2)}, u32[]{:S(2)}) collective-permute-start(f32[2,2,2,8,128]{4,1,3,2,0:T(2,128)} %copy.379), channel_id=1, source_target_pairs={{1,0},{2,1},{3,2},{4,3},{5,4},{6,5},{7,6},{8,7},{9,8},{10,9},{11,1... | collective-permute-start | bytes 98312 | tf_op jit(solution)/shard_map/ppermute | solution.py:21
  10.0 77.4 %all-to-all-start = ((s32[32,2,1]{1,2,0:T(1,128)}), s32[32,2,1]{1,2,0:T(1,128)}, u32[]{:S(2)}, u32[]{:S(2)}) async-start(s32[32,2,1]{1,2,0:T(1,128)} %bitcast.97), calls=%async_computation | async-start | bytes 32768 | tf_op jit(solution)/shard_map/all_to_all | solution.py:122
  68.5 6.5 copy-start.1
  70.5 1.3 copy-start.72
  70.5 1.9 copy-start.68
  70.5 1.9 copy-start.73
  71.3 3.0 copy-start.44
  83.1 2.1 copy-start.11
  90.0 1.8 copy-start.52
  90.0 1.8 copy-start.53
  90.8 1.0 copy-start.33
  90.8 1.1 copy-start.34
  136.8 6.1 collective-permute-start.2
  138.1 5.3 collective-permute-start.3
  142.9 1.5 copy-start.28
  142.9 1.5 copy-start.29
  142.9 1.5 copy-start.38
  142.9 1.5 copy-start.39
  143.4 1.0 copy-start.57
  143.4 1.0 copy-start.58
  143.4 1.0 copy-start.61
  193.5 6.1 collective-permute-start.4
  194.8 5.3 collective-permute-start.5
  199.6 1.5 copy-start.20
  199.6 1.5 copy-start.30
  199.6 1.5 copy-start.31
  199.6 1.5 copy-start.40
  199.6 1.5 copy-start.41
  253.0 6.1 collective-permute-start.6
  254.3 5.3 collective-permute-start.7
  259.1 1.5 copy-start.15
  259.1 1.5 copy-start.21
  259.1 1.5 copy-start.22
  259.1 1.5 copy-start.37
  312.5 43.5 %copy-start.9 = (f32[32,4,256]{2,1,0:T(4,128)S(1)}, f32[32,4,256]{2,1,0:T(4,128)}, u32[]{:S(2)}) copy-start(f32[32,4,256]{2,1,0:T(4,128)} %param.13) | copy-start | bytes 393220
  358.0 16.9 %all-to-all-start.1 = ((f32[64,4,4]{2,1,0:T(4,128)}), f32[64,4,4]{2,1,0:T(4,128)S(1)}, u32[]{:S(2)}, u32[]{:S(2)}) async-start(f32[64,4,4]{2,1,0:T(4,128)} %copy.269), calls=%async_computation.1 | async-start | bytes 262144 | tf_op jit(solution)/shard_map/all_to_all | solution.py:121
  366.3 10.1 %copy-start.27 = (f32[2,2,8,8,126]{4,1,3,2,0:T(2,128)S(1)}, f32[2,2,8,8,126]{4,1,3,2,0:T(2,128)}, u32[]{:S(2)}) copy-start(f32[2,2,8,8,126]{4,1,3,2,0:T(2,128)} %get-tuple-element.142) | copy-start | bytes 387076
  366.3 10.0 %collective-permute-start.9 = (f32[2,2,2,8,128]{4,1,3,2,0:T(2,128)}, f32[2,2,2,8,128]{4,1,3,2,0:T(2,128)}, u32[]{:S(2)}, u32[]{:S(2)}) collective-permute-start(f32[2,2,2,8,128]{4,1,3,2,0:T(2,128)} %get-tuple-element.127), channel_id=1, source_target_pairs={{0,1},{1,2},{2,3},{3,4},{4,5},{5,6},{6,7},{7,8},{8,9},{9,10},{10,1... | collective-permute-start | bytes 98312 | tf_op jit(solution)/shard_map/ppermute | solution.py:18
  370.2 6.2 collective-permute-start.8
  425.5 7.5 collective-permute-start.10
  426.8 6.2 collective-permute-start.11
  432.9 1.1 copy-start.12
  433.0 1.1 copy-start.13
  433.0 1.1 copy-start.16
  433.0 1.1 copy-start.17
  487.2 7.7 %collective-permute-start.12 = (f32[2,2,2,8,128]{4,1,3,2,0:T(2,128)}, f32[2,2,2,8,128]{4,1,3,2,0:T(2,128)}, u32[]{:S(2)}, u32[]{:S(2)}) collective-permute-start(f32[2,2,2,8,128]{4,1,3,2,0:T(2,128)} %get-tuple-element.84), channel_id=1, source_target_pairs={{1,0},{2,1},{3,2},{4,3},{5,4},{6,5},{7,6},{8,7},{9,8},{10,9},{11,1... | collective-permute-start | bytes 98312 | tf_op jit(solution)/shard_map/ppermute | solution.py:21
  488.5 6.4 collective-permute-start.13
  494.8 1.1 copy-start.14
  494.8 1.1 copy-start.18
  494.8 1.1 copy-start.19
  494.8 1.1 copy-start.23
  545.3 6.1 collective-permute-start.14
  546.6 5.3 collective-permute-start.15
  551.3 1.5 copy-start.35
  551.4 1.5 copy-start.36
  551.9 1.0 copy-start.59
  551.9 1.0 copy-start.60
  598.6 11.2 %slice-start = ((f32[4,4,4]{2,0,1:T(4,128)}), f32[4,3,4]{2,0,1:T(4,128)S(1)}, s32[]{:S(2)}) async-start(f32[4,4,4]{2,0,1:T(4,128)} %copy-done.51), calls=%async_computation.3 | async-start | bytes 12288 | tf_op jit(solution)/shard_map/slice | solution.py:131
  598.6 11.2 %copy-start.66 = (f32[4,1,4]{2,0,1:T(4,128)S(1)}, f32[4,1,4]{2,0,1:T(4,128)}, u32[]{:S(2)}) copy-start(f32[4,1,4]{2,0,1:T(4,128)} %slice.1403) | copy-start | bytes 196
  598.6 20.7 %all-to-all-start.2 = ((f32[64,4,4]{2,1,0:T(4,128)}), f32[64,4,4]{2,1,0:T(4,128)S(1)}, u32[]{:S(2)}, u32[]{:S(2)}) async-start(f32[64,4,4]{2,1,0:T(4,128)} %copy.273), calls=%async_computation.2 | async-start | bytes 262144 | tf_op jit(solution)/shard_map/all_to_all | solution.py:121
  610.0 9.3 %copy-start.65 = (s32[64]{0:T(128)S(1)}, s32[64]{0:T(128)}, u32[]{:S(2)}) copy-start(s32[64]{0:T(128)} %eq.29) | copy-start | bytes 772
  (33 other events, 26.2 us)
